TPU v7x, 32 devices: a whole 2x2x4 slice. The times are simulated.
32 devices in a mesh: blk: 8 (over z, x), cent: 4 (over y, core).
Axes of the slice: x: 2, y: 2, z: 4, core: 2. Of those that a mesh axis runs over, the one named last changes fastest.
Arguments:
- descriptors: bfloat16 [6144, 1024], P('blk'), may hold values from -6 to 6
- landmarks: bfloat16 [4096, 1024], P('blk'), may hold values from -6 to 6
- whitening: bfloat16 [4096, 4096], P('blk', 'cent'), may hold values from -0.09375 to 0.09375
- centroids: bfloat16 [4096, 4096], P('cent'), may hold values from -8 to 8, as said below
Outputs:
- assign: bfloat16 [6144, 4096], P('blk', 'cent')
- new_centroids: float32 [4096, 4096], P('blk', 'cent')
Inputs may be any that keep to these rules, and one draw needn't show every extreme that they name: `centroids`: centroid coordinates.
All inputs are finite; a program needn't handle non-finite values.
Results may differ from a plain program's by a relative error of at most 0.03.
Values may be sent and summed in bfloat16 or wider, within the bound.
No kernel may reach another device: no remote copies, remote signals or barrier semaphores. Data moves between devices by JAX's collectives and lax.ppermute only.
A program may use at most 128 MiB of HBM per device.

v0:
```python
import math
import jax
import jax.numpy as jnp
from jax import lax
from jax.sharding import PartitionSpec as P


def unit_rows(values):
    wide = values.astype(jnp.float32)
    sum_sq = jnp.sum(wide * wide, axis=1, keepdims=True)
    scale = lax.rsqrt(sum_sq + 1e-06)
    return (wide * scale).astype(jnp.bfloat16)


def per_device(descriptors, landmarks, whitening, centroids):
    unit_desc = unit_rows(descriptors)
    unit_land = unit_rows(landmarks)
    sharpness = math.sqrt(descriptors.shape[1])
    cosine = lax.dot_general(
        unit_desc,
        lax.all_gather(unit_land, "blk", axis=0, tiled=True),
        (((1,), (1,)), ((), ())),
        preferred_element_type=jnp.float32,
    )
    kernel = jnp.exp(sharpness * cosine).astype(jnp.bfloat16)
    feature_cols = jnp.dot(
        kernel,
        lax.all_gather(whitening, "blk", axis=0, tiled=True),
        preferred_element_type=jnp.float32,
    )
    features = lax.all_gather(feature_cols.astype(jnp.bfloat16), "cent", axis=1, tiled=True)
    logits = lax.dot_general(
        features, centroids, (((1,), (1,)), ((), ())), preferred_element_type=jnp.float32
    )
    local_top = jnp.max(logits, axis=1)
    row_top = lax.pmax(local_top, "cent")
    weights = jnp.exp(logits - row_top[:, None])
    row_total = lax.psum(jnp.sum(weights, axis=1), "cent")
    assign = (weights / row_total[:, None]).astype(jnp.bfloat16)
    counts = lax.psum(jnp.sum(assign.astype(jnp.float32), axis=0), "blk")
    sums = lax.psum_scatter(
        lax.dot_general(
            features, assign, (((0,), (0,)), ((), ())), preferred_element_type=jnp.float32
        ).astype(jnp.bfloat16),
        "blk",
        scatter_dimension=0,
        tiled=True,
    ).astype(jnp.float32)
    return (assign, sums / jnp.maximum(counts, 1.0)[None, :])


def solution(mesh):
    in_specs = (P("blk", None), P("blk", None), P("blk", "cent"), P("cent", None))
    out_specs = (P("blk", "cent"), P("blk", "cent"))
    return jax.shard_map(
        per_device, mesh=mesh, in_specs=in_specs, out_specs=out_specs, check_vma=False
    )
```

profile of v0, /device:TPU:0, one launch (start us, length us, event | category | flops | bytes accessed | tf_op | source)
XLA Modules:
  0.0 523.7 jit_solution(12697928453037709906)
XLA Ops:
  7.2 0.0 copy-start
  7.2 0.0 all-gather.6.cloned.1.call-start
  7.2 0.7 all-gather.6.cloned.1.call-update
  7.9 0.0 all-gather.4.cloned.1.call-start
  8.0 1.5 fusion.3
  9.5 2.4 fusion.4
  11.9 0.0 all-gather.4.cloned.1.call-update
  11.9 0.0 all-gather.8.cloned.1.call-start
  12.0 0.0 copy-done
  12.0 0.4 fusion
  12.4 125.0 %all-gather.6.cloned.1.call-done = bf16[4096,1024]{1,0:T(8,128)(2,1)} async-done(((bf16[512,1024]{1,0:T(8,128)(2,1)}), bf16[4096,1024]{1,0:T(8,128)(2,1)}) %all-gather.6.cloned.1.call-update) | async-done | bytes 8388624 | tf_op jit(solution)/shard_map/all_gather | solution.py:28
  137.3 125.4 %all-gather.4.cloned.1.call-done = bf16[4096,1024]{1,0:T(8,128)(2,1)} async-done(((bf16[512,1024]{1,0:T(8,128)(2,1)}), bf16[4096,1024]{1,0:T(8,128)(2,1)}) %all-gather.4.cloned.1.call-update) | async-done | bytes 8388624 | tf_op jit(solution)/shard_map/all_gather | solution.py:21
  262.7 20.2 %convolution_convert_fusion.1 = bf16[768,1024]{1,0:T(8,128)(2,1)} fusion(bf16[4096,1024]{1,0:T(8,128)(2,1)} %all-gather.6.cloned.1.call-done, bf16[4096,1024]{1,0:T(8,128)(2,1)} %all-gather.4.cloned.1.call-done, bf16[768,1024]{1,0:T(8,128)(2,1)S(1)} %copy-done, f32[768]{0:T(1024)S(1)} %add_rsqrt_fusion), kind=kOutput, calls=%fused_computation.15 | convolution fusion | flops 12894339072 | bytes 19926016 | tf_op jit(solution)/shard_map/dot_general | solution.py:26
  282.9 0.0 all-gather.8.cloned.1.call-update
  282.9 0.2 reduce-scatter.2.cloned.1.call-start
  283.1 44.5 %all-gather.8.cloned.1.call-done = bf16[768,4096]{1,0:T(8,128)(2,1)} async-done(((bf16[768,1024]{1,0:T(8,128)(2,1)}), bf16[768,4096]{1,0:T(8,128)(2,1)}) %all-gather.8.cloned.1.call-update) | async-done | bytes 6291472 | tf_op jit(solution)/shard_map/all_gather | solution.py:31
  327.6 11.1 %fusion.11 = (f32[768]{0:T(1024)S(1)}, f32[768,1024]{1,0:T(8,128)S(1)}) fusion(bf16[768,4096]{1,0:T(8,128)(2,1)} %all-gather.8.cloned.1.call-done, bf16[1024,4096]{1,0:T(8,128)(2,1)} %param.7), kind=kOutput, calls=%fused_computation.21 | convolution fusion | flops 6443236352 | bytes 17828864 | tf_op jit(solution)/shard_map/dot_general | solution.py:32
  338.7 5.9 %pmax.7 = f32[768]{0:T(1024)S(1)} all-reduce(f32[768]{0:T(1024)S(1)} %get-tuple-element.4), channel_id=1, replica_groups=mesh['blk'=8,'cent'=4] {'cent'}, use_global_device_ids=true, to_apply=%region_3.0 | all-reduce | flops 768 | bytes 6144 | tf_op jit(solution)/shard_map/pmax | solution.py:36
  344.6 0.9 fusion.2
  345.6 5.7 %psum.14 = f32[768]{0:T(1024)S(1)} all-reduce(f32[768]{0:T(1024)S(1)} %fusion.2), channel_id=1, replica_groups=mesh['blk'=8,'cent'=4] {'cent'}, use_global_device_ids=true, to_apply=%region_5.0 | all-reduce | flops 768 | bytes 6144 | tf_op jit(solution)/shard_map/psum | solution.py:38
  351.2 1.0 convert_reduce_fusion
  352.2 0.0 copy-start.1
  352.2 1.1 copy-done.1
  353.4 11.9 %convolution_convert_fusion = bf16[4096,1024]{1,0:T(8,128)(2,1)} fusion(bf16[768,4096]{1,0:T(8,128)(2,1)} %all-gather.8.cloned.1.call-done, bf16[768,1024]{1,0:T(8,128)(2,1)S(1)} %get-tuple-element.3), kind=kOutput, calls=%fused_computation.1 | convolution fusion | flops 6446645248 | bytes 16252928 | tf_op jit(solution)/shard_map/dot_general | solution.py:42
  365.2 0.0 reduce-scatter.2.cloned.1.call-update
  365.3 22.1 %psum.15 = f32[1024]{0:T(1024)S(1)} all-reduce(f32[1024]{0:T(1024)S(1)} %get-tuple-element.2), channel_id=1, replica_groups=mesh['blk'=8,'cent'=4] {'blk'}, use_global_device_ids=true, to_apply=%region_8.0 | all-reduce | flops 1024 | bytes 8192 | tf_op jit(solution)/shard_map/psum | solution.py:40
  387.4 127.0 %reduce-scatter.2.cloned.1.call-done = bf16[512,1024]{1,0:T(8,128)(2,1)} async-done(((bf16[4096,1024]{1,0:T(8,128)(2,1)}), bf16[512,1024]{1,0:T(8,128)(2,1)}) %reduce-scatter.2.cloned.1.call-update) | async-done | bytes 1048592 | tf_op jit(solution)/shard_map/reduce_scatter | solution.py:41
  514.3 2.9 convert_divide_fusion
  (3 shorter events, 0.0 us)
Async XLA Ops:
  7.2 4.8 copy-start
  7.2 130.2 %all-gather.6.cloned.1.call-start = ((), (), s32[]{:S(2)}) async-start(), calls=%async_computation.2 | async-start | bytes 9437184 | tf_op jit(solution)/shard_map/all_gather | solution.py:28
  7.9 254.8 %all-gather.4.cloned.1.call-start = ((), (), s32[]{:S(2)}) async-start(), calls=%async_computation.1 | async-start | bytes 9437184 | tf_op jit(solution)/shard_map/all_gather | solution.py:21
  11.9 315.7 %all-gather.8.cloned.1.call-start = ((), (), s32[]{:S(2)}) async-start(), calls=%async_computation.3 | async-start | bytes 7864320 | tf_op jit(solution)/shard_map/all_gather | solution.py:31
  282.9 231.4 %reduce-scatter.2.cloned.1.call-start = ((), (), s32[]{:S(2)}) async-start(), calls=%async_computation.4 | async-start | bytes 9437184 | tf_op jit(solution)/shard_map/reduce_scatter | solution.py:41
  352.2 1.1 copy-start.1
Sparse Core Ops, SparseCore 0:
  10.1 127.1 all-gather.5
  140.0 122.6 all-gather.3
  283.0 44.5 all-gather.7
  365.4 148.9 reduce-scatter.1
where the time goes:
time: 524 us
  waiting for transfers between devices  423 us (81%)
  matrix products  43.2 us (8%)
  blocking collectives  33.7 us (6%)
  between operations  13.8 us (3%)
  other arithmetic  9.08 us (2%)
    reduce_scatter x1, waiting for transfers between devices, per_device(): lax.psum_scatter(lax.dot_general(features, assign, (((0,), (0,)), ((), ()...  127 us
    all_gather x1, waiting for transfers between devices, per_device(): lax.all_gather(unit_land, 'blk', axis=0, tiled=True)  125 us
    all_gather x1, waiting for transfers between devices, per_device(): lax.all_gather(whitening, 'blk', axis=0, tiled=True)  125 us
    all_gather x1, waiting for transfers between devices, per_device(): lax.all_gather(feature_cols.astype(jnp.bfloat16), 'cent', axis=1, tiled=T...  44.5 us
    psum x1, blocking collectives, per_device(): counts = lax.psum(jnp.sum(assign.astype(jnp.float32), axis=0), 'blk')  22.1 us
    dot_general x1, matrix products, per_device(): jnp.dot(kernel, lax.all_gather(whitening, 'blk', axis=0, tiled=True), pre...  20.2 us
    dot_general x1, matrix products, per_device(): lax.dot_general(features, assign, (((0,), (0,)), ((), ())), preferred_ele...  11.9 us
    dot_general x1, matrix products, per_device(): lax.dot_general(features, centroids, (((1,), (1,)), ((), ())), preferred_...  11.1 us
  transfers between devices with their start and end apart: 4, of which 4 were waited for; matrix products, arithmetic and copies ran while one was open for 1% of the time, Pallas kernels for 0%

commit v1 on v0

--- a/solution.py
+++ b/solution.py
@@ -37,7 +37,8 @@
     weights = jnp.exp(logits - row_top[:, None])
     row_total = lax.psum(jnp.sum(weights, axis=1), "cent")
     assign = (weights / row_total[:, None]).astype(jnp.bfloat16)
-    counts = lax.psum(jnp.sum(assign.astype(jnp.float32), axis=0), "blk")
+    x_in = jnp.sum(assign.astype(jnp.float32), axis=0)
+    counts = jax.lax.all_gather(x_in, "blk").sum(axis=0)
     sums = lax.psum_scatter(
         lax.dot_general(
             features, assign, (((0,), (0,)), ((), ())), preferred_element_type=jnp.float32

time: 524 us -> 524 us (level)
  waiting for transfers between devices: 423 us -> 413 us
  blocking collectives: 33.7 us -> 43.4 us
    all_gather x0 -> x1, blocking collectives: none -> 31.8 us  [per_device(): counts = jax.lax.all_gather(x_in, 'blk').sum(axis=0)]
    psum x1 -> x0, blocking collectives: 22.1 us -> none  [per_device(): counts = lax.psum(jnp.sum(assign.astype(jnp.float32), axis=0), 'blk')]
    reduce_scatter x1, waiting for transfers between devices: 127 us -> 117 us  [per_device(): lax.psum_scatter(lax.dot_general(features, assign, (((0,), (0,)), ((), ()...]
where the time goes in v1:
time: 524 us
  waiting for transfers between devices  413 us (79%)
  blocking collectives  43.4 us (8%)
  matrix products  43.2 us (8%)
  between operations  13.8 us (3%)
  other arithmetic  9.1 us (2%)
    all_gather x1, waiting for transfers between devices, per_device(): lax.all_gather(unit_land, 'blk', axis=0, tiled=True)  125 us
    all_gather x1, waiting for transfers between devices, per_device(): lax.all_gather(whitening, 'blk', axis=0, tiled=True)  125 us
    reduce_scatter x1, waiting for transfers between devices, per_device(): lax.psum_scatter(lax.dot_general(features, assign, (((0,), (0,)), ((), ()...  117 us
    all_gather x1, waiting for transfers between devices, per_device(): lax.all_gather(feature_cols.astype(jnp.bfloat16), 'cent', axis=1, tiled=T...  44.5 us
    all_gather x1, blocking collectives, per_device(): counts = jax.lax.all_gather(x_in, 'blk').sum(axis=0)  31.8 us
    dot_general x1, matrix products, per_device(): jnp.dot(kernel, lax.all_gather(whitening, 'blk', axis=0, tiled=True), pre...  20.2 us
    dot_general x1, matrix products, per_device(): lax.dot_general(features, assign, (((0,), (0,)), ((), ())), preferred_ele...  11.9 us
    dot_general x1, matrix products, per_device(): lax.dot_general(features, centroids, (((1,), (1,)), ((), ())), preferred_...  11.1 us
  transfers between devices with their start and end apart: 4, of which 4 were waited for; matrix products, arithmetic and copies ran while one was open for 1% of the time, Pallas kernels for 0%

profile of v1, /device:TPU:0, one launch (start us, length us, event | category | flops | bytes accessed | tf_op | source)
XLA Modules:
  0.0 523.8 jit_solution(13222251277046482189)
XLA Ops:
  7.2 0.0 copy-start
  7.2 0.0 all-gather.7.cloned.1.call-start
  7.2 0.7 all-gather.7.cloned.1.call-update
  7.9 0.0 all-gather.5.cloned.1.call-start
  8.0 1.5 fusion.3
  9.5 2.4 fusion.4
  11.9 0.0 all-gather.5.cloned.1.call-update
  11.9 0.0 all-gather.9.cloned.1.call-start
  12.0 0.0 copy-done
  12.0 0.4 fusion
  12.4 125.0 %all-gather.7.cloned.1.call-done = bf16[4096,1024]{1,0:T(8,128)(2,1)} async-done(((bf16[512,1024]{1,0:T(8,128)(2,1)}), bf16[4096,1024]{1,0:T(8,128)(2,1)}) %all-gather.7.cloned.1.call-update) | async-done | bytes 8388624 | tf_op jit(solution)/shard_map/all_gather | solution.py:28
  137.3 125.4 %all-gather.5.cloned.1.call-done = bf16[4096,1024]{1,0:T(8,128)(2,1)} async-done(((bf16[512,1024]{1,0:T(8,128)(2,1)}), bf16[4096,1024]{1,0:T(8,128)(2,1)}) %all-gather.5.cloned.1.call-update) | async-done | bytes 8388624 | tf_op jit(solution)/shard_map/all_gather | solution.py:21
  262.7 20.2 %convolution_convert_fusion.1 = bf16[768,1024]{1,0:T(8,128)(2,1)} fusion(bf16[4096,1024]{1,0:T(8,128)(2,1)} %all-gather.7.cloned.1.call-done, bf16[4096,1024]{1,0:T(8,128)(2,1)} %all-gather.5.cloned.1.call-done, bf16[768,1024]{1,0:T(8,128)(2,1)S(1)} %copy-done, f32[768]{0:T(1024)S(1)} %add_rsqrt_fusion), kind=kOutput, calls=%fused_computation.15 | convolution fusion | flops 12894339072 | bytes 19926016 | tf_op jit(solution)/shard_map/dot_general | solution.py:26
  282.9 0.0 all-gather.9.cloned.1.call-update
  282.9 0.2 reduce-scatter.2.cloned.1.call-start
  283.1 44.5 %all-gather.9.cloned.1.call-done = bf16[768,4096]{1,0:T(8,128)(2,1)} async-done(((bf16[768,1024]{1,0:T(8,128)(2,1)}), bf16[768,4096]{1,0:T(8,128)(2,1)}) %all-gather.9.cloned.1.call-update) | async-done | bytes 6291472 | tf_op jit(solution)/shard_map/all_gather | solution.py:31
  327.6 11.1 %fusion.11 = (f32[768]{0:T(1024)S(1)}, f32[768,1024]{1,0:T(8,128)S(1)}) fusion(bf16[768,4096]{1,0:T(8,128)(2,1)} %all-gather.9.cloned.1.call-done, bf16[1024,4096]{1,0:T(8,128)(2,1)} %param.7), kind=kOutput, calls=%fused_computation.21 | convolution fusion | flops 6443236352 | bytes 17828864 | tf_op jit(solution)/shard_map/dot_general | solution.py:32
  338.7 5.9 %pmax.7 = f32[768]{0:T(1024)S(1)} all-reduce(f32[768]{0:T(1024)S(1)} %get-tuple-element.4), channel_id=1, replica_groups=mesh['blk'=8,'cent'=4] {'cent'}, use_global_device_ids=true, to_apply=%region_3.0 | all-reduce | flops 768 | bytes 6144 | tf_op jit(solution)/shard_map/pmax | solution.py:36
  344.6 0.9 fusion.2
  345.6 5.7 %psum.7 = f32[768]{0:T(1024)S(1)} all-reduce(f32[768]{0:T(1024)S(1)} %fusion.2), channel_id=1, replica_groups=mesh['blk'=8,'cent'=4] {'cent'}, use_global_device_ids=true, to_apply=%region_5.0 | all-reduce | flops 768 | bytes 6144 | tf_op jit(solution)/shard_map/psum | solution.py:38
  351.2 1.0 convert_reduce_fusion
  352.2 0.0 copy-start.1
  352.2 1.1 copy-done.1
  353.4 11.9 %convolution_convert_fusion = bf16[4096,1024]{1,0:T(8,128)(2,1)} fusion(bf16[768,4096]{1,0:T(8,128)(2,1)} %all-gather.9.cloned.1.call-done, bf16[768,1024]{1,0:T(8,128)(2,1)S(1)} %get-tuple-element.3), kind=kOutput, calls=%fused_computation.1 | convolution fusion | flops 6446645248 | bytes 16252928 | tf_op jit(solution)/shard_map/dot_general | solution.py:43
  365.2 0.0 reduce-scatter.2.cloned.1.call-update
  365.3 31.8 %all-gather = f32[8192]{0:T(1024)S(1)} all-gather(f32[1024]{0:T(1024)S(1)} %get-tuple-element.2), channel_id=2, replica_groups=mesh['blk'=8,'cent'=4] {'blk'}, dimensions={0}, use_global_device_ids=true | all-gather | bytes 36864 | tf_op jit(solution)/shard_map/all_gather | solution.py:41
  397.1 117.3 %reduce-scatter.2.cloned.1.call-done = bf16[512,1024]{1,0:T(8,128)(2,1)} async-done(((bf16[4096,1024]{1,0:T(8,128)(2,1)}), bf16[512,1024]{1,0:T(8,128)(2,1)}) %reduce-scatter.2.cloned.1.call-update) | async-done | bytes 1048592 | tf_op jit(solution)/shard_map/reduce_scatter | solution.py:42
  514.4 2.9 convert_divide_fusion
  (5 shorter events, 0.0 us)
Async XLA Ops:
  7.2 4.8 copy-start
  7.2 130.2 %all-gather.7.cloned.1.call-start = ((), (), s32[]{:S(2)}) async-start(), calls=%async_computation.2 | async-start | bytes 9437184 | tf_op jit(solution)/shard_map/all_gather | solution.py:28
  7.9 254.8 %all-gather.5.cloned.1.call-start = ((), (), s32[]{:S(2)}) async-start(), calls=%async_computation.1 | async-start | bytes 9437184 | tf_op jit(solution)/shard_map/all_gather | solution.py:21
  11.9 315.7 %all-gather.9.cloned.1.call-start = ((), (), s32[]{:S(2)}) async-start(), calls=%async_computation.3 | async-start | bytes 7864320 | tf_op jit(solution)/shard_map/all_gather | solution.py:31
  282.9 231.5 %reduce-scatter.2.cloned.1.call-start = ((), (), s32[]{:S(2)}) async-start(), calls=%async_computation.4 | async-start | bytes 9437184 | tf_op jit(solution)/shard_map/reduce_scatter | solution.py:42
  352.2 1.1 copy-start.1
Sparse Core Ops, SparseCore 0:
  10.1 127.1 all-gather.6
  140.0 122.6 all-gather.4
  283.0 44.5 all-gather.8
  365.4 148.9 reduce-scatter.1
